TPU v7x, 512 devices: a whole 4x4x16 slice. The times are simulated.
512 devices in a mesh: cand: 8 (over y, core), doc: 64 (over z, x).
Axes of the slice: x: 4, y: 4, z: 16, core: 2. Of those that a mesh axis runs over, the one named last changes fastest.
Arguments:
- queries: bfloat16 [8192, 8192], P('doc'), may hold values from -6 to 50
- keys_values: bfloat16 [2, 8192, 1024], P(None, 'doc', 'cand'), may hold values from -6 to 50
- factors: float32 [8, 64], P('cand'), may hold values from 1 to 16
- lengths: int32 [16], replicated, may hold values from 1 to 1024, 8192 in all
Outputs:
- attended: bfloat16 [8, 8192, 8192], P('cand', 'doc')
All inputs are finite; a program needn't handle non-finite values.
Results may differ from a plain program's by a relative error of at most 0.0053.
Values may be sent and summed in bfloat16 or wider, within the bound.
No kernel may reach another device: no remote copies, remote signals or barrier semaphores. Data moves between devices by JAX's collectives and lax.ppermute only.
A program may use at most 64 MiB of HBM per device.

v0:
```python
import math
import jax
import jax.numpy as jnp
from jax import lax
from jax.sharding import PartitionSpec as P

H = 64
KVH = 8
HD = 128
SPAN = 8
ROPE_BASE = 500000.0


def passed_along(value, axis, steps):
    count = lax.axis_size(axis)
    first, last = (max(0, -steps), min(count, count - steps))
    return lax.ppermute(value, axis, [(source, source + steps) for source in range(first, last)])


def locate(index_rows, lengths):
    ends = jnp.cumsum(lengths)
    starts = ends - lengths
    docid = jnp.sum((index_rows[:, None] >= ends[None, :]).astype(jnp.int32), axis=1)
    onehot = docid[:, None] == jnp.arange(lengths.shape[0], dtype=jnp.int32)[None, :]
    first_row = jnp.sum(jnp.where(onehot, starts[None, :], 0), axis=1)
    valid = index_rows >= 0
    return (jnp.where(valid, docid, -1), jnp.where(valid, index_rows - first_row, 0))


def rotate(values, offsets, factor):
    row_count = values.shape[0]
    heads_here = values.shape[1] // HD
    half_dim = HD // 2
    shaped = values.reshape(row_count, heads_here, HD).astype(jnp.float32)
    inverse = jnp.power(ROPE_BASE, -2.0 * jnp.arange(half_dim, dtype=jnp.float32) / HD) / factor
    angles = offsets.astype(jnp.float32)[:, None] * inverse[None, :]
    cosine = jnp.cos(angles)[:, None, :]
    sine = jnp.sin(angles)[:, None, :]
    first_half = shaped[..., :half_dim]
    second_half = shaped[..., half_dim:]
    turned = jnp.concatenate(
        [first_half * cosine - second_half * sine, second_half * cosine + first_half * sine],
        axis=-1,
    )
    return turned.reshape(row_count, heads_here * HD).astype(jnp.bfloat16)


def attend_group(query_rot, key_rot, value_rows, allowed):
    row_count = query_rot.shape[0]
    group_size = H // KVH
    q_part = query_rot.reshape(row_count, group_size, HD)
    scale = 1.0 / math.sqrt(HD)
    scores = jnp.einsum("rgd,wd->rgw", q_part, key_rot, preferred_element_type=jnp.float32) * scale
    scores = jnp.where(allowed[:, None, :], scores, -1e30)
    largest = jnp.max(scores, axis=-1, keepdims=True)
    expw = jnp.exp(scores - largest)
    total = jnp.sum(expw, axis=-1, keepdims=True)
    weights = expw.astype(jnp.bfloat16)
    numer = jnp.einsum("rgw,wd->rgd", weights, value_rows, preferred_element_type=jnp.float32)
    return (numer / total).astype(jnp.bfloat16).reshape(row_count, group_size * HD)


def on_device(queries, keys_values, factors, lengths):
    row_count = queries.shape[0]
    group_width = queries.shape[1] // KVH
    device = lax.axis_index("doc")
    group = lax.axis_index("cand")
    query_index = device * row_count + jnp.arange(row_count, dtype=jnp.int32)
    key_index = (device - SPAN) * row_count + jnp.arange((SPAN + 1) * row_count, dtype=jnp.int32)
    every_factor = lax.all_gather(factors, "cand", axis=0, tiled=True)
    pieces = []
    for distance in range(SPAN, 0, -1):
        pieces.append(passed_along(keys_values, "doc", distance))
    pieces.append(keys_values)
    window = jnp.concatenate(pieces, axis=1)
    query_doc, query_offset = locate(query_index, lengths)
    key_doc, key_offset = locate(key_index, lengths)
    allowed = (
        (key_doc[None, :] == query_doc[:, None])
        & (key_index[None, :] <= query_index[:, None])
        & (key_doc[None, :] >= 0)
    )
    own_queries = lax.dynamic_slice_in_dim(queries, group * group_width, group_width, 1)

    def per_candidate(factor):
        query_rot = rotate(own_queries, query_offset, factor)
        key_rot = rotate(window[0], key_offset, factor)
        return attend_group(query_rot, key_rot, window[1], allowed)

    mixed = lax.map(per_candidate, every_factor)
    return lax.all_to_all(mixed, "cand", 0, 2, tiled=True)


def solution(mesh):
    placed = (P("doc", None), P(None, "doc", "cand"), P("cand", None), P())
    return jax.shard_map(
        on_device, mesh=mesh, in_specs=placed, out_specs=P("cand", "doc", None), check_vma=False
    )
```

profile of v0, /device:TPU:32, one launch (start us, length us, event | category | flops | bytes accessed | tf_op | source)
XLA Modules:
  0.0 206.3 jit_solution(13450548175812455790)
XLA Ops:
  0.0 1.1 copy.37
  1.1 5.2 %collective-permute-start = (bf16[2,128,128]{1,2,0:T(8,128)(2,1)S(1)}, bf16[2,128,128]{1,2,0:T(8,128)(2,1)S(1)}, u32[]{:S(2)}, u32[]{:S(2)}) collective-permute-start(bf16[2,128,128]{1,2,0:T(8,128)(2,1)S(1)} %copy.37), channel_id=1, source_target_pairs={{0,8},{1,9},{2,10},{3,11},{4,12},{5,13},{6,14},{7,15},{8,16},{9,17... | collective-permute-start | bytes 196616 | tf_op jit(solution)/shard_map/ppermute | solution.py:17
  6.3 7.2 %collective-permute-start.1 = (bf16[2,128,128]{1,2,0:T(8,128)(2,1)S(1)}, bf16[2,128,128]{1,2,0:T(8,128)(2,1)S(1)}, u32[]{:S(2)}, u32[]{:S(2)}) collective-permute-start(bf16[2,128,128]{1,2,0:T(8,128)(2,1)S(1)} %copy.37), channel_id=1, source_target_pairs={{0,7},{1,8},{2,9},{3,10},{4,11},{5,12},{6,13},{7,14},{8,15},{9,16}... | collective-permute-start | bytes 196616 | tf_op jit(solution)/shard_map/ppermute | solution.py:17
  13.5 5.4 %collective-permute-start.2 = (bf16[2,128,128]{1,2,0:T(8,128)(2,1)S(1)}, bf16[2,128,128]{1,2,0:T(8,128)(2,1)S(1)}, u32[]{:S(2)}, u32[]{:S(2)}) collective-permute-start(bf16[2,128,128]{1,2,0:T(8,128)(2,1)S(1)} %copy.37), channel_id=1, source_target_pairs={{0,6},{1,7},{2,8},{3,9},{4,10},{5,11},{6,12},{7,13},{8,14},{9,15},... | collective-permute-start | bytes 196616 | tf_op jit(solution)/shard_map/ppermute | solution.py:17
  19.0 4.1 %collective-permute-start.3 = (bf16[2,128,128]{1,2,0:T(8,128)(2,1)S(1)}, bf16[2,128,128]{1,2,0:T(8,128)(2,1)S(1)}, u32[]{:S(2)}, u32[]{:S(2)}) collective-permute-start(bf16[2,128,128]{1,2,0:T(8,128)(2,1)S(1)} %copy.37), channel_id=1, source_target_pairs={{0,5},{1,6},{2,7},{3,8},{4,9},{5,10},{6,11},{7,12},{8,13},{9,14},{... | collective-permute-start | bytes 196616 | tf_op jit(solution)/shard_map/ppermute | solution.py:17
  23.1 5.0 %collective-permute-start.4 = (bf16[2,128,128]{1,2,0:T(8,128)(2,1)S(1)}, bf16[2,128,128]{1,2,0:T(8,128)(2,1)S(1)}, u32[]{:S(2)}, u32[]{:S(2)}) collective-permute-start(bf16[2,128,128]{1,2,0:T(8,128)(2,1)S(1)} %copy.37), channel_id=1, source_target_pairs={{0,4},{1,5},{2,6},{3,7},{4,8},{5,9},{6,10},{7,11},{8,12},{9,13},{1... | collective-permute-start | bytes 196616 | tf_op jit(solution)/shard_map/ppermute | solution.py:17
  32.0 11.5 %all-gather = f32[8,1,64]{2,1,0:T(1,128)} all-gather(f32[1,1,64]{2,1,0:T(1,128)} %bitcast.51), channel_id=1, replica_groups=mesh['cand'=8,'doc'=64] {'cand'}, dimensions={0}, use_global_device_ids=true | all-gather | bytes 2304 | tf_op jit(solution)/shard_map/all_gather | solution.py:70
  43.6 4.7 %collective-permute-start.5 = (bf16[2,128,128]{1,2,0:T(8,128)(2,1)S(1)}, bf16[2,128,128]{1,2,0:T(8,128)(2,1)S(1)}, u32[]{:S(2)}, u32[]{:S(2)}) collective-permute-start(bf16[2,128,128]{1,2,0:T(8,128)(2,1)S(1)} %copy.37), channel_id=1, source_target_pairs={{0,3},{1,4},{2,5},{3,6},{4,7},{5,8},{6,9},{7,10},{8,11},{9,12},{10... | collective-permute-start | bytes 196616 | tf_op jit(solution)/shard_map/ppermute | solution.py:17
  48.3 3.4 %collective-permute-start.6 = (bf16[2,128,128]{1,2,0:T(8,128)(2,1)S(1)}, bf16[2,128,128]{1,2,0:T(8,128)(2,1)S(1)}, u32[]{:S(2)}, u32[]{:S(2)}) collective-permute-start(bf16[2,128,128]{1,2,0:T(8,128)(2,1)S(1)} %copy.37), channel_id=1, source_target_pairs={{0,2},{1,3},{2,4},{3,5},{4,6},{5,7},{6,8},{7,9},{8,10},{9,11},{10,... | collective-permute-start | bytes 196616 | tf_op jit(solution)/shard_map/ppermute | solution.py:17
  51.8 1.9 collective-permute-start.7
  53.9 3.0 %collective-permute-done.6 = bf16[2,128,128]{1,2,0:T(8,128)(2,1)S(1)} collective-permute-done((bf16[2,128,128]{1,2,0:T(8,128)(2,1)S(1)}, bf16[2,128,128]{1,2,0:T(8,128)(2,1)S(1)}, u32[]{:S(2)}, u32[]{:S(2)}) %collective-permute-start.6) | collective-permute-done | bytes 65568 | tf_op jit(solution)/shard_map/ppermute | solution.py:17
  56.9 3.1 %collective-permute-done.7 = bf16[2,128,128]{1,2,0:T(8,128)(2,1)S(1)} collective-permute-done((bf16[2,128,128]{1,2,0:T(8,128)(2,1)S(1)}, bf16[2,128,128]{1,2,0:T(8,128)(2,1)S(1)}, u32[]{:S(2)}, u32[]{:S(2)}) %collective-permute-start.7) | collective-permute-done | bytes 65568 | tf_op jit(solution)/shard_map/ppermute | solution.py:17
  60.9 109.5 %while.13 = (s32[]{:T(128)}, bf16[8,128,1024]{1,2,0:T(8,128)(2,1)}, bf16[128,1024]{0,1:T(8,128)(2,1)S(1)}, f32[128,1]{0,1:T(1,128)S(1)}, f32[8,64]{1,0:T(8,128)}...) while((s32[]{:T(128)}, bf16[8,128,1024]{1,2,0:T(8,128)(2,1)}, ...), condition=%wide.region_8.9_spmd.clone, body=%wide.region_5.8_spmd.clone.sunk | while | flops 615544960 | bytes 23285628 | solution.py:90
  62.9 1.1 copy.56
  64.1 0.9 subtract_convert_fusion.2
  65.0 1.0 bitcast_convert_fusion.2
  66.7 1.9 fusion.47
  69.5 2.3 %fusion.49 = (f32[128,8]{0,1:T(8,128)S(1)}, f32[128,8,1152]{2,0,1:T(8,128)S(1)}) fusion(bf16[1152,1,64]{0,2,1:T(8,128)(2,1)S(1)} %get-tuple-element.261, bf16[1152,1,64]{0,2,1:T(8,128)(2,1)S(1)} %get-tuple-element.262, bf16[128,8,64]{2,0,1:T(8,128)(2,1)} %get-tuple-element.267, bf16[128,8,64]{2,0,1:T(8,128)(2,1)} %get-tuple-element.268, ...), kind=kOutput, calls=%fused_computation.66.clone.1 | convolution fusion | flops 306641920 | bytes 5427200 | tf_op jit(solution)/shard_map/while/body/eval_jaxpr/rgd,wd->rgw/dot_general | solution.py:53
  71.8 1.0 fusion.50
  72.8 1.0 fusion.51
  76.6 1.1 copy.56
  78.7 1.0 bitcast_convert_fusion.2
  80.4 1.9 fusion.47
  83.2 2.3 %fusion.49 = (f32[128,8]{0,1:T(8,128)S(1)}, f32[128,8,1152]{2,0,1:T(8,128)S(1)}) fusion(bf16[1152,1,64]{0,2,1:T(8,128)(2,1)S(1)} %get-tuple-element.261, bf16[1152,1,64]{0,2,1:T(8,128)(2,1)S(1)} %get-tuple-element.262, bf16[128,8,64]{2,0,1:T(8,128)(2,1)} %get-tuple-element.267, bf16[128,8,64]{2,0,1:T(8,128)(2,1)} %get-tuple-element.268, ...), kind=kOutput, calls=%fused_computation.66.clone.1 | convolution fusion | flops 306641920 | bytes 5427200 | tf_op jit(solution)/shard_map/while/body/eval_jaxpr/rgd,wd->rgw/dot_general | solution.py:53
  85.5 1.0 fusion.50
  86.5 1.0 fusion.51
  90.3 1.1 copy.56
  92.4 1.0 bitcast_convert_fusion.2
  94.1 1.9 fusion.47
  96.9 2.3 %fusion.49 = (f32[128,8]{0,1:T(8,128)S(1)}, f32[128,8,1152]{2,0,1:T(8,128)S(1)}) fusion(bf16[1152,1,64]{0,2,1:T(8,128)(2,1)S(1)} %get-tuple-element.261, bf16[1152,1,64]{0,2,1:T(8,128)(2,1)S(1)} %get-tuple-element.262, bf16[128,8,64]{2,0,1:T(8,128)(2,1)} %get-tuple-element.267, bf16[128,8,64]{2,0,1:T(8,128)(2,1)} %get-tuple-element.268, ...), kind=kOutput, calls=%fused_computation.66.clone.1 | convolution fusion | flops 306641920 | bytes 5427200 | tf_op jit(solution)/shard_map/while/body/eval_jaxpr/rgd,wd->rgw/dot_general | solution.py:53
  99.2 1.0 fusion.50
  100.2 1.0 fusion.51
  104.0 1.1 copy.56
  106.0 1.0 bitcast_convert_fusion.2
  107.8 1.9 fusion.47
  110.6 2.3 %fusion.49 = (f32[128,8]{0,1:T(8,128)S(1)}, f32[128,8,1152]{2,0,1:T(8,128)S(1)}) fusion(bf16[1152,1,64]{0,2,1:T(8,128)(2,1)S(1)} %get-tuple-element.261, bf16[1152,1,64]{0,2,1:T(8,128)(2,1)S(1)} %get-tuple-element.262, bf16[128,8,64]{2,0,1:T(8,128)(2,1)} %get-tuple-element.267, bf16[128,8,64]{2,0,1:T(8,128)(2,1)} %get-tuple-element.268, ...), kind=kOutput, calls=%fused_computation.66.clone.1 | convolution fusion | flops 306641920 | bytes 5427200 | tf_op jit(solution)/shard_map/while/body/eval_jaxpr/rgd,wd->rgw/dot_general | solution.py:53
  112.9 1.0 fusion.50
  113.9 1.0 fusion.51
  117.6 1.1 copy.56
  119.7 1.0 bitcast_convert_fusion.2
  121.4 1.9 fusion.47
  124.3 2.3 %fusion.49 = (f32[128,8]{0,1:T(8,128)S(1)}, f32[128,8,1152]{2,0,1:T(8,128)S(1)}) fusion(bf16[1152,1,64]{0,2,1:T(8,128)(2,1)S(1)} %get-tuple-element.261, bf16[1152,1,64]{0,2,1:T(8,128)(2,1)S(1)} %get-tuple-element.262, bf16[128,8,64]{2,0,1:T(8,128)(2,1)} %get-tuple-element.267, bf16[128,8,64]{2,0,1:T(8,128)(2,1)} %get-tuple-element.268, ...), kind=kOutput, calls=%fused_computation.66.clone.1 | convolution fusion | flops 306641920 | bytes 5427200 | tf_op jit(solution)/shard_map/while/body/eval_jaxpr/rgd,wd->rgw/dot_general | solution.py:53
  126.6 1.0 fusion.50
  127.6 1.0 fusion.51
  131.3 1.1 copy.56
  133.4 1.0 bitcast_convert_fusion.2
  135.1 1.9 fusion.47
  138.0 2.3 %fusion.49 = (f32[128,8]{0,1:T(8,128)S(1)}, f32[128,8,1152]{2,0,1:T(8,128)S(1)}) fusion(bf16[1152,1,64]{0,2,1:T(8,128)(2,1)S(1)} %get-tuple-element.261, bf16[1152,1,64]{0,2,1:T(8,128)(2,1)S(1)} %get-tuple-element.262, bf16[128,8,64]{2,0,1:T(8,128)(2,1)} %get-tuple-element.267, bf16[128,8,64]{2,0,1:T(8,128)(2,1)} %get-tuple-element.268, ...), kind=kOutput, calls=%fused_computation.66.clone.1 | convolution fusion | flops 306641920 | bytes 5427200 | tf_op jit(solution)/shard_map/while/body/eval_jaxpr/rgd,wd->rgw/dot_general | solution.py:53
  140.2 1.0 fusion.50
  141.3 1.0 fusion.51
  145.0 1.1 copy.56
  147.1 1.0 bitcast_convert_fusion.2
  148.8 1.9 fusion.47
  151.6 2.3 %fusion.49 = (f32[128,8]{0,1:T(8,128)S(1)}, f32[128,8,1152]{2,0,1:T(8,128)S(1)}) fusion(bf16[1152,1,64]{0,2,1:T(8,128)(2,1)S(1)} %get-tuple-element.261, bf16[1152,1,64]{0,2,1:T(8,128)(2,1)S(1)} %get-tuple-element.262, bf16[128,8,64]{2,0,1:T(8,128)(2,1)} %get-tuple-element.267, bf16[128,8,64]{2,0,1:T(8,128)(2,1)} %get-tuple-element.268, ...), kind=kOutput, calls=%fused_computation.66.clone.1 | convolution fusion | flops 306641920 | bytes 5427200 | tf_op jit(solution)/shard_map/while/body/eval_jaxpr/rgd,wd->rgw/dot_general | solution.py:53
  153.9 1.0 fusion.50
  154.9 1.0 fusion.51
  158.7 1.1 copy.56
  160.8 1.0 bitcast_convert_fusion.2
  162.5 1.9 fusion.47
  165.3 2.3 %fusion.49 = (f32[128,8]{0,1:T(8,128)S(1)}, f32[128,8,1152]{2,0,1:T(8,128)S(1)}) fusion(bf16[1152,1,64]{0,2,1:T(8,128)(2,1)S(1)} %get-tuple-element.261, bf16[1152,1,64]{0,2,1:T(8,128)(2,1)S(1)} %get-tuple-element.262, bf16[128,8,64]{2,0,1:T(8,128)(2,1)} %get-tuple-element.267, bf16[128,8,64]{2,0,1:T(8,128)(2,1)} %get-tuple-element.268, ...), kind=kOutput, calls=%fused_computation.66.clone.1 | convolution fusion | flops 306641920 | bytes 5427200 | tf_op jit(solution)/shard_map/while/body/eval_jaxpr/rgd,wd->rgw/dot_general | solution.py:53
  167.6 1.0 fusion.50
  168.6 1.0 fusion.51
  170.4 31.8 %all_to_all.18 = bf16[8,128,1024]{1,2,0:T(8,128)(2,1)} all-to-all(bf16[8,128,1024]{1,2,0:T(8,128)(2,1)} %get-tuple-element.110), channel_id=1, replica_groups=mesh['cand'=8,'doc'=64] {'cand'}, dimensions={0} | all-to-all | bytes 4194304 | tf_op jit(solution)/shard_map/all_to_all | solution.py:91
  202.2 4.1 %copy.48 = bf16[1,128,8192]{2,1,0:T(8,128)(2,1)} copy(bf16[1,128,8192]{1,2,0:T(8,128)(2,1)} %bitcast.47) | data formatting | bytes 4194304 | tf_op jit(solution)/shard_map/all_to_all | solution.py:91
  (165 shorter events, 45.5 us)
Async XLA Ops:
  0.0 31.8 %copy-start = (bf16[128,8192]{1,0:T(8,128)(2,1)S(1)}, bf16[128,8192]{1,0:T(8,128)(2,1)}, u32[]{:S(2)}) copy-start(bf16[128,8192]{1,0:T(8,128)(2,1)} %param.6) | copy-start | bytes 6291460
  1.1 42.5 %collective-permute-start = (bf16[2,128,128]{1,2,0:T(8,128)(2,1)S(1)}, bf16[2,128,128]{1,2,0:T(8,128)(2,1)S(1)}, u32[]{:S(2)}, u32[]{:S(2)}) collective-permute-start(bf16[2,128,128]{1,2,0:T(8,128)(2,1)S(1)} %copy.37), channel_id=1, source_target_pairs={{0,8},{1,9},{2,10},{3,11},{4,12},{5,13},{6,14},{7,15},{8,16},{9,17... | collective-permute-start | bytes 196616 | tf_op jit(solution)/shard_map/ppermute | solution.py:17
  6.3 42.0 %collective-permute-start.1 = (bf16[2,128,128]{1,2,0:T(8,128)(2,1)S(1)}, bf16[2,128,128]{1,2,0:T(8,128)(2,1)S(1)}, u32[]{:S(2)}, u32[]{:S(2)}) collective-permute-start(bf16[2,128,128]{1,2,0:T(8,128)(2,1)S(1)} %copy.37), channel_id=1, source_target_pairs={{0,7},{1,8},{2,9},{3,10},{4,11},{5,12},{6,13},{7,14},{8,15},{9,16}... | collective-permute-start | bytes 196616 | tf_op jit(solution)/shard_map/ppermute | solution.py:17
  13.5 38.3 %collective-permute-start.2 = (bf16[2,128,128]{1,2,0:T(8,128)(2,1)S(1)}, bf16[2,128,128]{1,2,0:T(8,128)(2,1)S(1)}, u32[]{:S(2)}, u32[]{:S(2)}) collective-permute-start(bf16[2,128,128]{1,2,0:T(8,128)(2,1)S(1)} %copy.37), channel_id=1, source_target_pairs={{0,6},{1,7},{2,8},{3,9},{4,10},{5,11},{6,12},{7,13},{8,14},{9,15},... | collective-permute-start | bytes 196616 | tf_op jit(solution)/shard_map/ppermute | solution.py:17
  19.0 34.8 %collective-permute-start.3 = (bf16[2,128,128]{1,2,0:T(8,128)(2,1)S(1)}, bf16[2,128,128]{1,2,0:T(8,128)(2,1)S(1)}, u32[]{:S(2)}, u32[]{:S(2)}) collective-permute-start(bf16[2,128,128]{1,2,0:T(8,128)(2,1)S(1)} %copy.37), channel_id=1, source_target_pairs={{0,5},{1,6},{2,7},{3,8},{4,9},{5,10},{6,11},{7,12},{8,13},{9,14},{... | collective-permute-start | bytes 196616 | tf_op jit(solution)/shard_map/ppermute | solution.py:17
  23.1 30.7 %collective-permute-start.4 = (bf16[2,128,128]{1,2,0:T(8,128)(2,1)S(1)}, bf16[2,128,128]{1,2,0:T(8,128)(2,1)S(1)}, u32[]{:S(2)}, u32[]{:S(2)}) collective-permute-start(bf16[2,128,128]{1,2,0:T(8,128)(2,1)S(1)} %copy.37), channel_id=1, source_target_pairs={{0,4},{1,5},{2,6},{3,7},{4,8},{5,9},{6,10},{7,11},{8,12},{9,13},{1... | collective-permute-start | bytes 196616 | tf_op jit(solution)/shard_map/ppermute | solution.py:17
  30.5 1.3 copy-start.4
  43.6 10.2 %collective-permute-start.5 = (bf16[2,128,128]{1,2,0:T(8,128)(2,1)S(1)}, bf16[2,128,128]{1,2,0:T(8,128)(2,1)S(1)}, u32[]{:S(2)}, u32[]{:S(2)}) collective-permute-start(bf16[2,128,128]{1,2,0:T(8,128)(2,1)S(1)} %copy.37), channel_id=1, source_target_pairs={{0,3},{1,4},{2,5},{3,6},{4,7},{5,8},{6,9},{7,10},{8,11},{9,12},{10... | collective-permute-start | bytes 196616 | tf_op jit(solution)/shard_map/ppermute | solution.py:17
  48.3 8.6 %collective-permute-start.6 = (bf16[2,128,128]{1,2,0:T(8,128)(2,1)S(1)}, bf16[2,128,128]{1,2,0:T(8,128)(2,1)S(1)}, u32[]{:S(2)}, u32[]{:S(2)}) collective-permute-start(bf16[2,128,128]{1,2,0:T(8,128)(2,1)S(1)} %copy.37), channel_id=1, source_target_pairs={{0,2},{1,3},{2,4},{3,5},{4,6},{5,7},{6,8},{7,9},{8,10},{9,11},{10,... | collective-permute-start | bytes 196616 | tf_op jit(solution)/shard_map/ppermute | solution.py:17
  51.8 8.3 %collective-permute-start.7 = (bf16[2,128,128]{1,2,0:T(8,128)(2,1)S(1)}, bf16[2,128,128]{1,2,0:T(8,128)(2,1)S(1)}, u32[]{:S(2)}, u32[]{:S(2)}) collective-permute-start(bf16[2,128,128]{1,2,0:T(8,128)(2,1)S(1)} %copy.37), channel_id=1, source_target_pairs={{0,1},{1,2},{2,3},{3,4},{4,5},{5,6},{6,7},{7,8},{8,9},{9,10},{10,1... | collective-permute-start | bytes 196616 | tf_op jit(solution)/shard_map/ppermute | solution.py:17
  60.1 0.8 copy-start.1
  60.9 1.0 copy-start.5
  61.6 1.1 copy-start.3
  69.5 3.3 %copy-start.2 = (bf16[2,1152,128]{1,2,0:T(8,128)(2,1)S(1)}, bf16[2,1152,128]{1,2,0:T(8,128)(2,1)}, u32[]{:S(2)}) copy-start(bf16[2,1152,128]{1,2,0:T(8,128)(2,1)} %get-tuple-element.304) | copy-start | bytes 1769476 | tf_op jit(solution)/shard_map/while
  71.8 2.8 %copy-start.6 = (f32[128,1]{0,1:T(1,128)S(1)}, f32[128,1]{0,1:T(1,128)}, u32[]{:S(2)}) copy-start(f32[128,1]{0,1:T(1,128)} %copy-done.5) | copy-start | bytes 1540 | tf_op jit(solution)/shard_map/while
  74.6 1.0 copy-start.5
  75.3 1.1 copy-start.3
  83.2 3.3 %copy-start.2 = (bf16[2,1152,128]{1,2,0:T(8,128)(2,1)S(1)}, bf16[2,1152,128]{1,2,0:T(8,128)(2,1)}, u32[]{:S(2)}) copy-start(bf16[2,1152,128]{1,2,0:T(8,128)(2,1)} %get-tuple-element.304) | copy-start | bytes 1769476 | tf_op jit(solution)/shard_map/while
  85.5 2.8 %copy-start.6 = (f32[128,1]{0,1:T(1,128)S(1)}, f32[128,1]{0,1:T(1,128)}, u32[]{:S(2)}) copy-start(f32[128,1]{0,1:T(1,128)} %copy-done.5) | copy-start | bytes 1540 | tf_op jit(solution)/shard_map/while
  88.3 1.0 copy-start.5
  89.0 1.1 copy-start.3
  96.9 3.3 %copy-start.2 = (bf16[2,1152,128]{1,2,0:T(8,128)(2,1)S(1)}, bf16[2,1152,128]{1,2,0:T(8,128)(2,1)}, u32[]{:S(2)}) copy-start(bf16[2,1152,128]{1,2,0:T(8,128)(2,1)} %get-tuple-element.304) | copy-start | bytes 1769476 | tf_op jit(solution)/shard_map/while
  99.2 2.8 %copy-start.6 = (f32[128,1]{0,1:T(1,128)S(1)}, f32[128,1]{0,1:T(1,128)}, u32[]{:S(2)}) copy-start(f32[128,1]{0,1:T(1,128)} %copy-done.5) | copy-start | bytes 1540 | tf_op jit(solution)/shard_map/while
  102.0 1.0 copy-start.5
  102.7 1.1 copy-start.3
  110.6 3.3 %copy-start.2 = (bf16[2,1152,128]{1,2,0:T(8,128)(2,1)S(1)}, bf16[2,1152,128]{1,2,0:T(8,128)(2,1)}, u32[]{:S(2)}) copy-start(bf16[2,1152,128]{1,2,0:T(8,128)(2,1)} %get-tuple-element.304) | copy-start | bytes 1769476 | tf_op jit(solution)/shard_map/while
  112.9 2.8 %copy-start.6 = (f32[128,1]{0,1:T(1,128)S(1)}, f32[128,1]{0,1:T(1,128)}, u32[]{:S(2)}) copy-start(f32[128,1]{0,1:T(1,128)} %copy-done.5) | copy-start | bytes 1540 | tf_op jit(solution)/shard_map/while
  115.7 1.0 copy-start.5
  116.4 1.1 copy-start.3
  124.3 3.3 %copy-start.2 = (bf16[2,1152,128]{1,2,0:T(8,128)(2,1)S(1)}, bf16[2,1152,128]{1,2,0:T(8,128)(2,1)}, u32[]{:S(2)}) copy-start(bf16[2,1152,128]{1,2,0:T(8,128)(2,1)} %get-tuple-element.304) | copy-start | bytes 1769476 | tf_op jit(solution)/shard_map/while
  126.5 2.8 %copy-start.6 = (f32[128,1]{0,1:T(1,128)S(1)}, f32[128,1]{0,1:T(1,128)}, u32[]{:S(2)}) copy-start(f32[128,1]{0,1:T(1,128)} %copy-done.5) | copy-start | bytes 1540 | tf_op jit(solution)/shard_map/while
  129.3 1.0 copy-start.5
  130.0 1.1 copy-start.3
  138.0 3.3 %copy-start.2 = (bf16[2,1152,128]{1,2,0:T(8,128)(2,1)S(1)}, bf16[2,1152,128]{1,2,0:T(8,128)(2,1)}, u32[]{:S(2)}) copy-start(bf16[2,1152,128]{1,2,0:T(8,128)(2,1)} %get-tuple-element.304) | copy-start | bytes 1769476 | tf_op jit(solution)/shard_map/while
  140.2 2.8 %copy-start.6 = (f32[128,1]{0,1:T(1,128)S(1)}, f32[128,1]{0,1:T(1,128)}, u32[]{:S(2)}) copy-start(f32[128,1]{0,1:T(1,128)} %copy-done.5) | copy-start | bytes 1540 | tf_op jit(solution)/shard_map/while
  143.0 1.0 copy-start.5
  143.7 1.1 copy-start.3
  151.6 3.3 %copy-start.2 = (bf16[2,1152,128]{1,2,0:T(8,128)(2,1)S(1)}, bf16[2,1152,128]{1,2,0:T(8,128)(2,1)}, u32[]{:S(2)}) copy-start(bf16[2,1152,128]{1,2,0:T(8,128)(2,1)} %get-tuple-element.304) | copy-start | bytes 1769476 | tf_op jit(solution)/shard_map/while
  153.9 2.8 %copy-start.6 = (f32[128,1]{0,1:T(1,128)S(1)}, f32[128,1]{0,1:T(1,128)}, u32[]{:S(2)}) copy-start(f32[128,1]{0,1:T(1,128)} %copy-done.5) | copy-start | bytes 1540 | tf_op jit(solution)/shard_map/while
  156.7 1.0 copy-start.5
  157.4 1.1 copy-start.3
  165.3 3.3 %copy-start.2 = (bf16[2,1152,128]{1,2,0:T(8,128)(2,1)S(1)}, bf16[2,1152,128]{1,2,0:T(8,128)(2,1)}, u32[]{:S(2)}) copy-start(bf16[2,1152,128]{1,2,0:T(8,128)(2,1)} %get-tuple-element.304) | copy-start | bytes 1769476 | tf_op jit(solution)/shard_map/while
  167.6 2.8 %copy-start.6 = (f32[128,1]{0,1:T(1,128)S(1)}, f32[128,1]{0,1:T(1,128)}, u32[]{:S(2)}) copy-start(f32[128,1]{0,1:T(1,128)} %copy-done.5) | copy-start | bytes 1540 | tf_op jit(solution)/shard_map/while
where the time goes:
time: 208 us; the launch traced here: 206 us
  other arithmetic  62.6 us (30%)
  blocking collectives  43.4 us (21%)
  starting transfers between devices  37.1 us (18%)
  local copies, waits for them, and re-layouts  29.7 us (14%)
  matrix products  26.4 us (13%)
  waiting for transfers between devices  6.2 us (3%)
    ppermute x8, starting transfers between devices, passed_along(): lax.ppermute(value, axis, [(source, source + steps) for source in range(f...  37.1 us
    all_to_all x1, blocking collectives, on_device(): return lax.all_to_all(mixed, 'cand', 0, 2, tiled=True)  31.8 us
    another operation x26, other arithmetic  28.7 us
    dot_general x8, matrix products, attend_group(): jnp.einsum('rgd,wd->rgw', q_part, key_rot, preferred_element_type=jnp.flo...  18.1 us
    all_gather x1, blocking collectives, on_device(): every_factor = lax.all_gather(factors, 'cand', axis=0, tiled=True)  11.5 us
    while x80, local copies, waits for them, and re-layouts  10.9 us
    dot_general x8, matrix products, attend_group(): jnp.einsum('rgw,wd->rgd', weights, value_rows, preferred_element_type=jnp...  8.29 us
    reduce_sum x8, other arithmetic, attend_group(): total = jnp.sum(expw, axis=-1, keepdims=True)  8.04 us
  transfers between devices with their start and end apart: 8, of which 2 were waited for; matrix products, arithmetic and copies ran while one was open for 2% of the time, Pallas kernels for 0%

commit v1 on v0

--- a/solution.py
+++ b/solution.py
@@ -9,6 +9,17 @@
 HD = 128
 SPAN = 8
 ROPE_BASE = 500000.0
+
+
+def gather_by_hops(shard, mesh_axis, dim):
+    size = lax.axis_size(mesh_axis)
+    right = [(i, (i + 1) % size) for i in range(size)]
+    parts = [shard]
+    for stride in range(1, size):
+        parts = [lax.ppermute(parts[0], mesh_axis, right), *parts]
+    out = jnp.concatenate(parts, axis=dim)
+    turn = (lax.axis_index(mesh_axis) + 1) * parts[-1].shape[dim]
+    return jnp.roll(out, turn, axis=dim)
 
 
 def passed_along(value, axis, steps):
@@ -67,7 +78,7 @@
     group = lax.axis_index("cand")
     query_index = device * row_count + jnp.arange(row_count, dtype=jnp.int32)
     key_index = (device - SPAN) * row_count + jnp.arange((SPAN + 1) * row_count, dtype=jnp.int32)
-    every_factor = lax.all_gather(factors, "cand", axis=0, tiled=True)
+    every_factor = gather_by_hops(factors, "cand", 0)
     pieces = []
     for distance in range(SPAN, 0, -1):
         pieces.append(passed_along(keys_values, "doc", distance))

time: 208 us -> 220 us (1.058)
  waiting for transfers between devices: 6.2 us -> 30.6 us
  blocking collectives: 43.4 us -> 31.8 us
  other arithmetic: 62.6 us -> 57.4 us
  local copies, waits for them, and re-layouts: 29.7 us -> 33.2 us
    ppermute x0 -> x7, waiting for transfers between devices: none -> 24.4 us  [gather_by_hops(): parts = [lax.ppermute(parts[0], mesh_axis, right), *parts]]
    all_gather x1 -> x0, blocking collectives: 11.5 us -> none  [on_device(): every_factor = lax.all_gather(factors, 'cand', axis=0, tiled=True)]
    mul x8, other arithmetic: 5.59 us -> 0.12 us  [rotate(): angles = offsets.astype(jnp.float32)[:, None] * inverse[None, :]]
    while x80 -> x112, local copies, waits for them, and re-layouts: 10.9 us -> 12.9 us
  transfers between devices with their start and end apart: 8 -> 15, of which waited for: 2 -> 9; matrix products, arithmetic and copies ran while one was open for 2% -> 2% of each run, Pallas kernels for 0% -> 0%
where the time goes in v1:
time: 220 us; the launch traced here: 219 us
  other arithmetic  57.4 us (26%)
  starting transfers between devices  38.1 us (17%)
  local copies, waits for them, and re-layouts  33.2 us (15%)
  blocking collectives  31.8 us (14%)
  waiting for transfers between devices  30.6 us (14%)
  matrix products  26.4 us (12%)
    ppermute x8, starting transfers between devices, passed_along(): lax.ppermute(value, axis, [(source, source + steps) for source in range(f...  37.1 us
    all_to_all x1, blocking collectives, on_device(): return lax.all_to_all(mixed, 'cand', 0, 2, tiled=True)  31.8 us
    another operation x26, other arithmetic  29 us
    ppermute x7, waiting for transfers between devices, gather_by_hops(): parts = [lax.ppermute(parts[0], mesh_axis, right), *parts]  24.4 us
    dot_general x8, matrix products, attend_group(): jnp.einsum('rgd,wd->rgw', q_part, key_rot, preferred_element_type=jnp.flo...  18.1 us
    while x112, local copies, waits for them, and re-layouts  12.9 us
    dot_general x8, matrix products, attend_group(): jnp.einsum('rgw,wd->rgd', weights, value_rows, preferred_element_type=jnp...  8.26 us
    reduce_sum x8, other arithmetic, attend_group(): total = jnp.sum(expw, axis=-1, keepdims=True)  8.04 us
  transfers between devices with their start and end apart: 15, of which 9 were waited for; matrix products, arithmetic and copies ran while one was open for 2% of the time, Pallas kernels for 0%

profile of v1, /device:TPU:32, one launch (start us, length us, event | category | flops | bytes accessed | tf_op | source)
XLA Modules:
  0.0 218.7 jit_solution(16919738389233541315)
XLA Ops:
  0.0 1.1 copy.31
  1.1 5.2 %collective-permute-start.7 = (bf16[2,128,128]{1,2,0:T(8,128)(2,1)S(1)}, bf16[2,128,128]{1,2,0:T(8,128)(2,1)S(1)}, u32[]{:S(2)}, u32[]{:S(2)}) collective-permute-start(bf16[2,128,128]{1,2,0:T(8,128)(2,1)S(1)} %copy.31), channel_id=1, source_target_pairs={{0,8},{1,9},{2,10},{3,11},{4,12},{5,13},{6,14},{7,15},{8,16},{9,17... | collective-permute-start | bytes 196616 | tf_op jit(solution)/shard_map/ppermute | solution.py:28
  6.3 7.2 %collective-permute-start.8 = (bf16[2,128,128]{1,2,0:T(8,128)(2,1)S(1)}, bf16[2,128,128]{1,2,0:T(8,128)(2,1)S(1)}, u32[]{:S(2)}, u32[]{:S(2)}) collective-permute-start(bf16[2,128,128]{1,2,0:T(8,128)(2,1)S(1)} %copy.31), channel_id=1, source_target_pairs={{0,7},{1,8},{2,9},{3,10},{4,11},{5,12},{6,13},{7,14},{8,15},{9,16}... | collective-permute-start | bytes 196616 | tf_op jit(solution)/shard_map/ppermute | solution.py:28
  13.5 5.4 %collective-permute-start.9 = (bf16[2,128,128]{1,2,0:T(8,128)(2,1)S(1)}, bf16[2,128,128]{1,2,0:T(8,128)(2,1)S(1)}, u32[]{:S(2)}, u32[]{:S(2)}) collective-permute-start(bf16[2,128,128]{1,2,0:T(8,128)(2,1)S(1)} %copy.31), channel_id=1, source_target_pairs={{0,6},{1,7},{2,8},{3,9},{4,10},{5,11},{6,12},{7,13},{8,14},{9,15},... | collective-permute-start | bytes 196616 | tf_op jit(solution)/shard_map/ppermute | solution.py:28
  19.0 4.1 %collective-permute-start.10 = (bf16[2,128,128]{1,2,0:T(8,128)(2,1)S(1)}, bf16[2,128,128]{1,2,0:T(8,128)(2,1)S(1)}, u32[]{:S(2)}, u32[]{:S(2)}) collective-permute-start(bf16[2,128,128]{1,2,0:T(8,128)(2,1)S(1)} %copy.31), channel_id=1, source_target_pairs={{0,5},{1,6},{2,7},{3,8},{4,9},{5,10},{6,11},{7,12},{8,13},{9,14},{... | collective-permute-start | bytes 196616 | tf_op jit(solution)/shard_map/ppermute | solution.py:28
  27.4 1.0 collective-permute-start.1
  28.5 3.1 %collective-permute-done.1 = f32[1,64]{1,0:T(1,128)S(1)} collective-permute-done((f32[1,64]{1,0:T(1,128)S(1)}, f32[1,64]{1,0:T(1,128)S(1)}, u32[]{:S(2)}, u32[]{:S(2)}) %collective-permute-start.1) | collective-permute-done | bytes 288 | tf_op jit(solution)/shard_map/ppermute | solution.py:19
  31.6 4.1 %collective-permute-done.2 = f32[1,64]{1,0:T(1,128)S(1)} collective-permute-done((f32[1,64]{1,0:T(1,128)S(1)}, f32[1,64]{1,0:T(1,128)S(1)}, u32[]{:S(2)}, u32[]{:S(2)}) %collective-permute-start.2) | collective-permute-done | bytes 288 | tf_op jit(solution)/shard_map/ppermute | solution.py:19
  35.8 4.2 %collective-permute-done.3 = f32[1,64]{1,0:T(1,128)S(1)} collective-permute-done((f32[1,64]{1,0:T(1,128)S(1)}, f32[1,64]{1,0:T(1,128)S(1)}, u32[]{:S(2)}, u32[]{:S(2)}) %collective-permute-start.3) | collective-permute-done | bytes 288 | tf_op jit(solution)/shard_map/ppermute | solution.py:19
  40.0 4.2 %collective-permute-done.4 = f32[1,64]{1,0:T(1,128)S(1)} collective-permute-done((f32[1,64]{1,0:T(1,128)S(1)}, f32[1,64]{1,0:T(1,128)S(1)}, u32[]{:S(2)}, u32[]{:S(2)}) %collective-permute-start.4) | collective-permute-done | bytes 288 | tf_op jit(solution)/shard_map/ppermute | solution.py:19
  44.1 4.2 %collective-permute-done.5 = f32[1,64]{1,0:T(1,128)S(1)} collective-permute-done((f32[1,64]{1,0:T(1,128)S(1)}, f32[1,64]{1,0:T(1,128)S(1)}, u32[]{:S(2)}, u32[]{:S(2)}) %collective-permute-start.5) | collective-permute-done | bytes 288 | tf_op jit(solution)/shard_map/ppermute | solution.py:19
  48.5 4.0 %collective-permute-done.6 = f32[1,64]{1,0:T(1,128)S(1)} collective-permute-done((f32[1,64]{1,0:T(1,128)S(1)}, f32[1,64]{1,0:T(1,128)S(1)}, u32[]{:S(2)}, u32[]{:S(2)}) %collective-permute-start.6) | collective-permute-done | bytes 288 | tf_op jit(solution)/shard_map/ppermute | solution.py:19
  52.5 5.0 %collective-permute-start.11 = (bf16[2,128,128]{1,2,0:T(8,128)(2,1)S(1)}, bf16[2,128,128]{1,2,0:T(8,128)(2,1)S(1)}, u32[]{:S(2)}, u32[]{:S(2)}) collective-permute-start(bf16[2,128,128]{1,2,0:T(8,128)(2,1)S(1)} %copy.31), channel_id=1, source_target_pairs={{0,4},{1,5},{2,6},{3,7},{4,8},{5,9},{6,10},{7,11},{8,12},{9,13},{1... | collective-permute-start | bytes 196616 | tf_op jit(solution)/shard_map/ppermute | solution.py:28
  57.5 1.4 concatenate.23
  58.9 4.7 %collective-permute-start.12 = (bf16[2,128,128]{1,2,0:T(8,128)(2,1)S(1)}, bf16[2,128,128]{1,2,0:T(8,128)(2,1)S(1)}, u32[]{:S(2)}, u32[]{:S(2)}) collective-permute-start(bf16[2,128,128]{1,2,0:T(8,128)(2,1)S(1)} %copy.31), channel_id=1, source_target_pairs={{0,3},{1,4},{2,5},{3,6},{4,7},{5,8},{6,9},{7,10},{8,11},{9,12},{10... | collective-permute-start | bytes 196616 | tf_op jit(solution)/shard_map/ppermute | solution.py:28
  63.7 3.4 %collective-permute-start.13 = (bf16[2,128,128]{1,2,0:T(8,128)(2,1)S(1)}, bf16[2,128,128]{1,2,0:T(8,128)(2,1)S(1)}, u32[]{:S(2)}, u32[]{:S(2)}) collective-permute-start(bf16[2,128,128]{1,2,0:T(8,128)(2,1)S(1)} %copy.31), channel_id=1, source_target_pairs={{0,2},{1,3},{2,4},{3,5},{4,6},{5,7},{6,8},{7,9},{8,10},{9,11},{10,... | collective-permute-start | bytes 196616 | tf_op jit(solution)/shard_map/ppermute | solution.py:28
  67.1 1.9 collective-permute-start.14
  69.2 3.0 %collective-permute-done.13 = bf16[2,128,128]{1,2,0:T(8,128)(2,1)S(1)} collective-permute-done((bf16[2,128,128]{1,2,0:T(8,128)(2,1)S(1)}, bf16[2,128,128]{1,2,0:T(8,128)(2,1)S(1)}, u32[]{:S(2)}, u32[]{:S(2)}) %collective-permute-start.13) | collective-permute-done | bytes 65568 | tf_op jit(solution)/shard_map/ppermute | solution.py:28
  72.3 3.2 %collective-permute-done.14 = bf16[2,128,128]{1,2,0:T(8,128)(2,1)S(1)} collective-permute-done((bf16[2,128,128]{1,2,0:T(8,128)(2,1)S(1)}, bf16[2,128,128]{1,2,0:T(8,128)(2,1)S(1)}, u32[]{:S(2)}, u32[]{:S(2)}) %collective-permute-start.14) | collective-permute-done | bytes 65568 | tf_op jit(solution)/shard_map/ppermute | solution.py:28
  76.3 106.5 %while.13 = (s32[]{:T(128)}, bf16[8,128,1024]{1,2,0:T(8,128)(2,1)}, bf16[128,1024]{0,1:T(8,128)(2,1)S(1)}, f32[128,1]{0,1:T(1,128)S(1)}, f32[8,64]{1,0:T(8,128)S...) while((s32[]{:T(128)}, bf16[8,128,1024]{1,2,0:T(8,128)(2,1)}, ...), condition=%wide.region_8.9_spmd.clone, body=%wide.region_5.8_spmd.clone.sunk | while | flops 615544960 | bytes 23302068 | solution.py:101
  77.8 1.1 copy.50
  80.0 1.0 bitcast_convert_fusion.2
  81.7 1.9 fusion.47
  84.5 2.3 %fusion.49 = (f32[128,8]{0,1:T(8,128)S(1)}, f32[128,8,1152]{2,0,1:T(8,128)S(1)}) fusion(bf16[1152,1,64]{0,2,1:T(8,128)(2,1)S(1)} %get-tuple-element.261, bf16[1152,1,64]{0,2,1:T(8,128)(2,1)S(1)} %get-tuple-element.262, bf16[128,8,64]{2,0,1:T(8,128)(2,1)} %get-tuple-element.267, bf16[128,8,64]{2,0,1:T(8,128)(2,1)} %get-tuple-element.268, ...), kind=kOutput, calls=%fused_computation.67.clone.1 | convolution fusion | flops 306641920 | bytes 5427200 | tf_op jit(solution)/shard_map/while/body/eval_jaxpr/rgd,wd->rgw/dot_general | solution.py:64
  86.8 1.0 fusion.50
  87.8 1.0 fusion.51
  91.2 1.1 copy.50
  93.3 1.0 bitcast_convert_fusion.2
  95.0 1.9 fusion.47
  97.8 2.3 %fusion.49 = (f32[128,8]{0,1:T(8,128)S(1)}, f32[128,8,1152]{2,0,1:T(8,128)S(1)}) fusion(bf16[1152,1,64]{0,2,1:T(8,128)(2,1)S(1)} %get-tuple-element.261, bf16[1152,1,64]{0,2,1:T(8,128)(2,1)S(1)} %get-tuple-element.262, bf16[128,8,64]{2,0,1:T(8,128)(2,1)} %get-tuple-element.267, bf16[128,8,64]{2,0,1:T(8,128)(2,1)} %get-tuple-element.268, ...), kind=kOutput, calls=%fused_computation.67.clone.1 | convolution fusion | flops 306641920 | bytes 5427200 | tf_op jit(solution)/shard_map/while/body/eval_jaxpr/rgd,wd->rgw/dot_general | solution.py:64
  100.1 1.0 fusion.50
  101.2 1.0 fusion.51
  104.5 1.1 copy.50
  108.3 1.9 fusion.47
  111.2 2.3 %fusion.49 = (f32[128,8]{0,1:T(8,128)S(1)}, f32[128,8,1152]{2,0,1:T(8,128)S(1)}) fusion(bf16[1152,1,64]{0,2,1:T(8,128)(2,1)S(1)} %get-tuple-element.261, bf16[1152,1,64]{0,2,1:T(8,128)(2,1)S(1)} %get-tuple-element.262, bf16[128,8,64]{2,0,1:T(8,128)(2,1)} %get-tuple-element.267, bf16[128,8,64]{2,0,1:T(8,128)(2,1)} %get-tuple-element.268, ...), kind=kOutput, calls=%fused_computation.67.clone.1 | convolution fusion | flops 306641920 | bytes 5427200 | tf_op jit(solution)/shard_map/while/body/eval_jaxpr/rgd,wd->rgw/dot_general | solution.py:64
  113.4 1.0 fusion.50
  114.5 1.0 fusion.51
  117.8 1.1 copy.50
  121.6 1.9 fusion.47
  124.5 2.3 %fusion.49 = (f32[128,8]{0,1:T(8,128)S(1)}, f32[128,8,1152]{2,0,1:T(8,128)S(1)}) fusion(bf16[1152,1,64]{0,2,1:T(8,128)(2,1)S(1)} %get-tuple-element.261, bf16[1152,1,64]{0,2,1:T(8,128)(2,1)S(1)} %get-tuple-element.262, bf16[128,8,64]{2,0,1:T(8,128)(2,1)} %get-tuple-element.267, bf16[128,8,64]{2,0,1:T(8,128)(2,1)} %get-tuple-element.268, ...), kind=kOutput, calls=%fused_computation.67.clone.1 | convolution fusion | flops 306641920 | bytes 5427200 | tf_op jit(solution)/shard_map/while/body/eval_jaxpr/rgd,wd->rgw/dot_general | solution.py:64
  126.8 1.0 fusion.50
  127.8 1.0 fusion.51
  131.1 1.1 copy.50
  134.9 1.9 fusion.47
  137.8 2.3 %fusion.49 = (f32[128,8]{0,1:T(8,128)S(1)}, f32[128,8,1152]{2,0,1:T(8,128)S(1)}) fusion(bf16[1152,1,64]{0,2,1:T(8,128)(2,1)S(1)} %get-tuple-element.261, bf16[1152,1,64]{0,2,1:T(8,128)(2,1)S(1)} %get-tuple-element.262, bf16[128,8,64]{2,0,1:T(8,128)(2,1)} %get-tuple-element.267, bf16[128,8,64]{2,0,1:T(8,128)(2,1)} %get-tuple-element.268, ...), kind=kOutput, calls=%fused_computation.67.clone.1 | convolution fusion | flops 306641920 | bytes 5427200 | tf_op jit(solution)/shard_map/while/body/eval_jaxpr/rgd,wd->rgw/dot_general | solution.py:64
  140.1 1.0 fusion.50
  141.1 1.0 fusion.51
  144.4 1.1 copy.50
  148.2 1.9 fusion.47
  151.1 2.3 %fusion.49 = (f32[128,8]{0,1:T(8,128)S(1)}, f32[128,8,1152]{2,0,1:T(8,128)S(1)}) fusion(bf16[1152,1,64]{0,2,1:T(8,128)(2,1)S(1)} %get-tuple-element.261, bf16[1152,1,64]{0,2,1:T(8,128)(2,1)S(1)} %get-tuple-element.262, bf16[128,8,64]{2,0,1:T(8,128)(2,1)} %get-tuple-element.267, bf16[128,8,64]{2,0,1:T(8,128)(2,1)} %get-tuple-element.268, ...), kind=kOutput, calls=%fused_computation.67.clone.1 | convolution fusion | flops 306641920 | bytes 5427200 | tf_op jit(solution)/shard_map/while/body/eval_jaxpr/rgd,wd->rgw/dot_general | solution.py:64
  153.4 1.0 fusion.50
  154.4 1.0 fusion.51
  157.7 1.1 copy.50
  161.6 1.9 fusion.47
  164.4 2.3 %fusion.49 = (f32[128,8]{0,1:T(8,128)S(1)}, f32[128,8,1152]{2,0,1:T(8,128)S(1)}) fusion(bf16[1152,1,64]{0,2,1:T(8,128)(2,1)S(1)} %get-tuple-element.261, bf16[1152,1,64]{0,2,1:T(8,128)(2,1)S(1)} %get-tuple-element.262, bf16[128,8,64]{2,0,1:T(8,128)(2,1)} %get-tuple-element.267, bf16[128,8,64]{2,0,1:T(8,128)(2,1)} %get-tuple-element.268, ...), kind=kOutput, calls=%fused_computation.67.clone.1 | convolution fusion | flops 306641920 | bytes 5427200 | tf_op jit(solution)/shard_map/while/body/eval_jaxpr/rgd,wd->rgw/dot_general | solution.py:64
  166.7 1.0 fusion.50
  167.7 1.0 fusion.51
  171.1 1.1 copy.50
  174.9 1.9 fusion.47
  177.7 2.3 %fusion.49 = (f32[128,8]{0,1:T(8,128)S(1)}, f32[128,8,1152]{2,0,1:T(8,128)S(1)}) fusion(bf16[1152,1,64]{0,2,1:T(8,128)(2,1)S(1)} %get-tuple-element.261, bf16[1152,1,64]{0,2,1:T(8,128)(2,1)S(1)} %get-tuple-element.262, bf16[128,8,64]{2,0,1:T(8,128)(2,1)} %get-tuple-element.267, bf16[128,8,64]{2,0,1:T(8,128)(2,1)} %get-tuple-element.268, ...), kind=kOutput, calls=%fused_computation.67.clone.1 | convolution fusion | flops 306641920 | bytes 5427200 | tf_op jit(solution)/shard_map/while/body/eval_jaxpr/rgd,wd->rgw/dot_general | solution.py:64
  180.0 1.0 fusion.50
  181.0 1.0 fusion.51
  182.8 31.8 %all_to_all.18 = bf16[8,128,1024]{1,2,0:T(8,128)(2,1)} all-to-all(bf16[8,128,1024]{1,2,0:T(8,128)(2,1)} %get-tuple-element.110), channel_id=1, replica_groups=mesh['cand'=8,'doc'=64] {'cand'}, dimensions={0} | all-to-all | bytes 4194304 | tf_op jit(solution)/shard_map/all_to_all | solution.py:102
  214.6 4.1 %copy.42 = bf16[1,128,8192]{2,1,0:T(8,128)(2,1)} copy(bf16[1,128,8192]{1,2,0:T(8,128)(2,1)} %bitcast.45) | data formatting | bytes 4194304 | tf_op jit(solution)/shard_map/all_to_all | solution.py:102
  (212 shorter events, 50.0 us)
Async XLA Ops:
  0.0 31.6 %copy-start = (bf16[128,8192]{1,0:T(8,128)(2,1)S(1)}, bf16[128,8192]{1,0:T(8,128)(2,1)}, u32[]{:S(2)}) copy-start(bf16[128,8192]{1,0:T(8,128)(2,1)} %param.6) | copy-start | bytes 6291460
  1.1 57.8 %collective-permute-start.7 = (bf16[2,128,128]{1,2,0:T(8,128)(2,1)S(1)}, bf16[2,128,128]{1,2,0:T(8,128)(2,1)S(1)}, u32[]{:S(2)}, u32[]{:S(2)}) collective-permute-start(bf16[2,128,128]{1,2,0:T(8,128)(2,1)S(1)} %copy.31), channel_id=1, source_target_pairs={{0,8},{1,9},{2,10},{3,11},{4,12},{5,13},{6,14},{7,15},{8,16},{9,17... | collective-permute-start | bytes 196616 | tf_op jit(solution)/shard_map/ppermute | solution.py:28
  6.3 57.4 %collective-permute-start.8 = (bf16[2,128,128]{1,2,0:T(8,128)(2,1)S(1)}, bf16[2,128,128]{1,2,0:T(8,128)(2,1)S(1)}, u32[]{:S(2)}, u32[]{:S(2)}) collective-permute-start(bf16[2,128,128]{1,2,0:T(8,128)(2,1)S(1)} %copy.31), channel_id=1, source_target_pairs={{0,7},{1,8},{2,9},{3,10},{4,11},{5,12},{6,13},{7,14},{8,15},{9,16}... | collective-permute-start | bytes 196616 | tf_op jit(solution)/shard_map/ppermute | solution.py:28
  13.5 53.6 %collective-permute-start.9 = (bf16[2,128,128]{1,2,0:T(8,128)(2,1)S(1)}, bf16[2,128,128]{1,2,0:T(8,128)(2,1)S(1)}, u32[]{:S(2)}, u32[]{:S(2)}) collective-permute-start(bf16[2,128,128]{1,2,0:T(8,128)(2,1)S(1)} %copy.31), channel_id=1, source_target_pairs={{0,6},{1,7},{2,8},{3,9},{4,10},{5,11},{6,12},{7,13},{8,14},{9,15},... | collective-permute-start | bytes 196616 | tf_op jit(solution)/shard_map/ppermute | solution.py:28
  19.0 50.1 %collective-permute-start.10 = (bf16[2,128,128]{1,2,0:T(8,128)(2,1)S(1)}, bf16[2,128,128]{1,2,0:T(8,128)(2,1)S(1)}, u32[]{:S(2)}, u32[]{:S(2)}) collective-permute-start(bf16[2,128,128]{1,2,0:T(8,128)(2,1)S(1)} %copy.31), channel_id=1, source_target_pairs={{0,5},{1,6},{2,7},{3,8},{4,9},{5,10},{6,11},{7,12},{8,13},{9,14},{... | collective-permute-start | bytes 196616 | tf_op jit(solution)/shard_map/ppermute | solution.py:28
  23.1 4.3 %collective-permute-start = (f32[1,64]{1,0:T(1,128)}, f32[1,64]{1,0:T(1,128)S(1)}, u32[]{:S(2)}, u32[]{:S(2)}) collective-permute-start(f32[1,64]{1,0:T(1,128)} %param.8), channel_id=1, source_target_pairs={{0,64},{64,128},{128,192},{192,256},{256,320},{320,384},{384,448},... | collective-permute-start | bytes 776 | tf_op jit(solution)/shard_map/ppermute | solution.py:19
  25.5 27.0 %copy-start.4 = (s32[128]{0:T(128)}, s32[128]{0:T(128)S(1)}, u32[]{:S(2)}) copy-start(s32[128]{0:T(128)S(1)} %iota_add_fusion.1) | copy-start | bytes 1540
  27.4 4.2 %collective-permute-start.1 = (f32[1,64]{1,0:T(1,128)S(1)}, f32[1,64]{1,0:T(1,128)S(1)}, u32[]{:S(2)}, u32[]{:S(2)}) collective-permute-start(f32[1,64]{1,0:T(1,128)S(1)} %collective-permute-done), channel_id=1, source_target_pairs={{0,64},{64,128},{128,192},{192,256},{256,320},{320,384},{384,448},... | collective-permute-start | bytes 776 | tf_op jit(solution)/shard_map/ppermute | solution.py:19
  31.6 4.2 %collective-permute-start.2 = (f32[1,64]{1,0:T(1,128)S(1)}, f32[1,64]{1,0:T(1,128)S(1)}, u32[]{:S(2)}, u32[]{:S(2)}) collective-permute-start(f32[1,64]{1,0:T(1,128)S(1)} %collective-permute-done.1), channel_id=1, source_target_pairs={{0,64},{64,128},{128,192},{192,256},{256,320},{320,384},{384,448},... | collective-permute-start | bytes 776 | tf_op jit(solution)/shard_map/ppermute | solution.py:19
  35.8 4.2 %collective-permute-start.3 = (f32[1,64]{1,0:T(1,128)S(1)}, f32[1,64]{1,0:T(1,128)S(1)}, u32[]{:S(2)}, u32[]{:S(2)}) collective-permute-start(f32[1,64]{1,0:T(1,128)S(1)} %collective-permute-done.2), channel_id=1, source_target_pairs={{0,64},{64,128},{128,192},{192,256},{256,320},{320,384},{384,448},... | collective-permute-start | bytes 776 | tf_op jit(solution)/shard_map/ppermute | solution.py:19
  40.0 4.2 %collective-permute-start.4 = (f32[1,64]{1,0:T(1,128)S(1)}, f32[1,64]{1,0:T(1,128)S(1)}, u32[]{:S(2)}, u32[]{:S(2)}) collective-permute-start(f32[1,64]{1,0:T(1,128)S(1)} %collective-permute-done.3), channel_id=1, source_target_pairs={{0,64},{64,128},{128,192},{192,256},{256,320},{320,384},{384,448},... | collective-permute-start | bytes 776 | tf_op jit(solution)/shard_map/ppermute | solution.py:19
  44.1 4.2 %collective-permute-start.5 = (f32[1,64]{1,0:T(1,128)S(1)}, f32[1,64]{1,0:T(1,128)S(1)}, u32[]{:S(2)}, u32[]{:S(2)}) collective-permute-start(f32[1,64]{1,0:T(1,128)S(1)} %collective-permute-done.4), channel_id=1, source_target_pairs={{0,64},{64,128},{128,192},{192,256},{256,320},{320,384},{384,448},... | collective-permute-start | bytes 776 | tf_op jit(solution)/shard_map/ppermute | solution.py:19
  48.3 4.2 %collective-permute-start.6 = (f32[1,64]{1,0:T(1,128)S(1)}, f32[1,64]{1,0:T(1,128)S(1)}, u32[]{:S(2)}, u32[]{:S(2)}) collective-permute-start(f32[1,64]{1,0:T(1,128)S(1)} %collective-permute-done.5), channel_id=1, source_target_pairs={{0,64},{64,128},{128,192},{192,256},{256,320},{320,384},{384,448},... | collective-permute-start | bytes 776 | tf_op jit(solution)/shard_map/ppermute | solution.py:19
  52.5 16.6 %collective-permute-start.11 = (bf16[2,128,128]{1,2,0:T(8,128)(2,1)S(1)}, bf16[2,128,128]{1,2,0:T(8,128)(2,1)S(1)}, u32[]{:S(2)}, u32[]{:S(2)}) collective-permute-start(bf16[2,128,128]{1,2,0:T(8,128)(2,1)S(1)} %copy.31), channel_id=1, source_target_pairs={{0,4},{1,5},{2,6},{3,7},{4,8},{5,9},{6,10},{7,11},{8,12},{9,13},{1... | collective-permute-start | bytes 196616 | tf_op jit(solution)/shard_map/ppermute | solution.py:28
  58.9 10.3 %collective-permute-start.12 = (bf16[2,128,128]{1,2,0:T(8,128)(2,1)S(1)}, bf16[2,128,128]{1,2,0:T(8,128)(2,1)S(1)}, u32[]{:S(2)}, u32[]{:S(2)}) collective-permute-start(bf16[2,128,128]{1,2,0:T(8,128)(2,1)S(1)} %copy.31), channel_id=1, source_target_pairs={{0,3},{1,4},{2,5},{3,6},{4,7},{5,8},{6,9},{7,10},{8,11},{9,12},{10... | collective-permute-start | bytes 196616 | tf_op jit(solution)/shard_map/ppermute | solution.py:28
  63.7 8.6 %collective-permute-start.13 = (bf16[2,128,128]{1,2,0:T(8,128)(2,1)S(1)}, bf16[2,128,128]{1,2,0:T(8,128)(2,1)S(1)}, u32[]{:S(2)}, u32[]{:S(2)}) collective-permute-start(bf16[2,128,128]{1,2,0:T(8,128)(2,1)S(1)} %copy.31), channel_id=1, source_target_pairs={{0,2},{1,3},{2,4},{3,5},{4,6},{5,7},{6,8},{7,9},{8,10},{9,11},{10,... | collective-permute-start | bytes 196616 | tf_op jit(solution)/shard_map/ppermute | solution.py:28
  67.1 8.3 %collective-permute-start.14 = (bf16[2,128,128]{1,2,0:T(8,128)(2,1)S(1)}, bf16[2,128,128]{1,2,0:T(8,128)(2,1)S(1)}, u32[]{:S(2)}, u32[]{:S(2)}) collective-permute-start(bf16[2,128,128]{1,2,0:T(8,128)(2,1)S(1)} %copy.31), channel_id=1, source_target_pairs={{0,1},{1,2},{2,3},{3,4},{4,5},{5,6},{6,7},{7,8},{8,9},{9,10},{10,1... | collective-permute-start | bytes 196616 | tf_op jit(solution)/shard_map/ppermute | solution.py:28
  75.5 0.8 copy-start.1
  76.3 0.6 copy-start.7
  76.3 1.3 copy-start.3
  84.5 3.3 %copy-start.2 = (bf16[2,1152,128]{1,2,0:T(8,128)(2,1)S(1)}, bf16[2,1152,128]{1,2,0:T(8,128)(2,1)}, u32[]{:S(2)}) copy-start(bf16[2,1152,128]{1,2,0:T(8,128)(2,1)} %get-tuple-element.304) | copy-start | bytes 1769476 | tf_op jit(solution)/shard_map/while
  86.8 2.8 %copy-start.6 = (f32[128,1]{0,1:T(1,128)S(1)}, f32[128,1]{0,1:T(1,128)}, u32[]{:S(2)}) copy-start(f32[128,1]{0,1:T(1,128)} %copy-done.5) | copy-start | bytes 1540 | tf_op jit(solution)/shard_map/while
  86.8 2.8 %copy-start.8 = (f32[8,64]{1,0:T(8,128)S(1)}, f32[8,64]{1,0:T(8,128)}, u32[]{:S(2)}) copy-start(f32[8,64]{1,0:T(8,128)} %copy-done.7) | copy-start | bytes 6148 | tf_op jit(solution)/shard_map/while
  89.6 0.5 copy-start.5
  89.6 0.6 copy-start.7
  89.6 1.3 copy-start.3
  97.8 3.3 %copy-start.2 = (bf16[2,1152,128]{1,2,0:T(8,128)(2,1)S(1)}, bf16[2,1152,128]{1,2,0:T(8,128)(2,1)}, u32[]{:S(2)}) copy-start(bf16[2,1152,128]{1,2,0:T(8,128)(2,1)} %get-tuple-element.304) | copy-start | bytes 1769476 | tf_op jit(solution)/shard_map/while
  100.1 2.8 %copy-start.6 = (f32[128,1]{0,1:T(1,128)S(1)}, f32[128,1]{0,1:T(1,128)}, u32[]{:S(2)}) copy-start(f32[128,1]{0,1:T(1,128)} %copy-done.5) | copy-start | bytes 1540 | tf_op jit(solution)/shard_map/while
  100.1 2.8 %copy-start.8 = (f32[8,64]{1,0:T(8,128)S(1)}, f32[8,64]{1,0:T(8,128)}, u32[]{:S(2)}) copy-start(f32[8,64]{1,0:T(8,128)} %copy-done.7) | copy-start | bytes 6148 | tf_op jit(solution)/shard_map/while
  102.9 0.5 copy-start.5
  102.9 0.6 copy-start.7
  103.0 1.3 copy-start.3
  111.2 3.3 %copy-start.2 = (bf16[2,1152,128]{1,2,0:T(8,128)(2,1)S(1)}, bf16[2,1152,128]{1,2,0:T(8,128)(2,1)}, u32[]{:S(2)}) copy-start(bf16[2,1152,128]{1,2,0:T(8,128)(2,1)} %get-tuple-element.304) | copy-start | bytes 1769476 | tf_op jit(solution)/shard_map/while
  113.4 2.8 %copy-start.6 = (f32[128,1]{0,1:T(1,128)S(1)}, f32[128,1]{0,1:T(1,128)}, u32[]{:S(2)}) copy-start(f32[128,1]{0,1:T(1,128)} %copy-done.5) | copy-start | bytes 1540 | tf_op jit(solution)/shard_map/while
  113.4 2.8 %copy-start.8 = (f32[8,64]{1,0:T(8,128)S(1)}, f32[8,64]{1,0:T(8,128)}, u32[]{:S(2)}) copy-start(f32[8,64]{1,0:T(8,128)} %copy-done.7) | copy-start | bytes 6148 | tf_op jit(solution)/shard_map/while
  116.2 0.5 copy-start.5
  116.2 0.6 copy-start.7
  116.3 1.3 copy-start.3
  124.5 3.3 %copy-start.2 = (bf16[2,1152,128]{1,2,0:T(8,128)(2,1)S(1)}, bf16[2,1152,128]{1,2,0:T(8,128)(2,1)}, u32[]{:S(2)}) copy-start(bf16[2,1152,128]{1,2,0:T(8,128)(2,1)} %get-tuple-element.304) | copy-start | bytes 1769476 | tf_op jit(solution)/shard_map/while
  126.7 2.8 %copy-start.6 = (f32[128,1]{0,1:T(1,128)S(1)}, f32[128,1]{0,1:T(1,128)}, u32[]{:S(2)}) copy-start(f32[128,1]{0,1:T(1,128)} %copy-done.5) | copy-start | bytes 1540 | tf_op jit(solution)/shard_map/while
  126.8 2.8 %copy-start.8 = (f32[8,64]{1,0:T(8,128)S(1)}, f32[8,64]{1,0:T(8,128)}, u32[]{:S(2)}) copy-start(f32[8,64]{1,0:T(8,128)} %copy-done.7) | copy-start | bytes 6148 | tf_op jit(solution)/shard_map/while
  129.6 0.6 copy-start.7
  129.6 1.3 copy-start.3
  137.8 3.3 %copy-start.2 = (bf16[2,1152,128]{1,2,0:T(8,128)(2,1)S(1)}, bf16[2,1152,128]{1,2,0:T(8,128)(2,1)}, u32[]{:S(2)}) copy-start(bf16[2,1152,128]{1,2,0:T(8,128)(2,1)} %get-tuple-element.304) | copy-start | bytes 1769476 | tf_op jit(solution)/shard_map/while
  140.1 2.8 %copy-start.6 = (f32[128,1]{0,1:T(1,128)S(1)}, f32[128,1]{0,1:T(1,128)}, u32[]{:S(2)}) copy-start(f32[128,1]{0,1:T(1,128)} %copy-done.5) | copy-start | bytes 1540 | tf_op jit(solution)/shard_map/while
  140.1 2.8 %copy-start.8 = (f32[8,64]{1,0:T(8,128)S(1)}, f32[8,64]{1,0:T(8,128)}, u32[]{:S(2)}) copy-start(f32[8,64]{1,0:T(8,128)} %copy-done.7) | copy-start | bytes 6148 | tf_op jit(solution)/shard_map/while
  142.9 0.5 copy-start.5
  142.9 0.6 copy-start.7
  142.9 1.3 copy-start.3
  151.1 3.3 %copy-start.2 = (bf16[2,1152,128]{1,2,0:T(8,128)(2,1)S(1)}, bf16[2,1152,128]{1,2,0:T(8,128)(2,1)}, u32[]{:S(2)}) copy-start(bf16[2,1152,128]{1,2,0:T(8,128)(2,1)} %get-tuple-element.304) | copy-start | bytes 1769476 | tf_op jit(solution)/shard_map/while
  153.4 2.8 %copy-start.6 = (f32[128,1]{0,1:T(1,128)S(1)}, f32[128,1]{0,1:T(1,128)}, u32[]{:S(2)}) copy-start(f32[128,1]{0,1:T(1,128)} %copy-done.5) | copy-start | bytes 1540 | tf_op jit(solution)/shard_map/while
  153.4 2.8 %copy-start.8 = (f32[8,64]{1,0:T(8,128)S(1)}, f32[8,64]{1,0:T(8,128)}, u32[]{:S(2)}) copy-start(f32[8,64]{1,0:T(8,128)} %copy-done.7) | copy-start | bytes 6148 | tf_op jit(solution)/shard_map/while
  156.2 0.5 copy-start.5
  156.2 0.6 copy-start.7
  156.2 1.3 copy-start.3
  164.4 3.3 %copy-start.2 = (bf16[2,1152,128]{1,2,0:T(8,128)(2,1)S(1)}, bf16[2,1152,128]{1,2,0:T(8,128)(2,1)}, u32[]{:S(2)}) copy-start(bf16[2,1152,128]{1,2,0:T(8,128)(2,1)} %get-tuple-element.304) | copy-start | bytes 1769476 | tf_op jit(solution)/shard_map/while
  166.7 2.8 %copy-start.6 = (f32[128,1]{0,1:T(1,128)S(1)}, f32[128,1]{0,1:T(1,128)}, u32[]{:S(2)}) copy-start(f32[128,1]{0,1:T(1,128)} %copy-done.5) | copy-start | bytes 1540 | tf_op jit(solution)/shard_map/while
  166.7 2.8 %copy-start.8 = (f32[8,64]{1,0:T(8,128)S(1)}, f32[8,64]{1,0:T(8,128)}, u32[]{:S(2)}) copy-start(f32[8,64]{1,0:T(8,128)} %copy-done.7) | copy-start | bytes 6148 | tf_op jit(solution)/shard_map/while
  169.5 0.5 copy-start.5
  169.5 0.6 copy-start.7
  169.5 1.3 copy-start.3
  177.7 3.3 %copy-start.2 = (bf16[2,1152,128]{1,2,0:T(8,128)(2,1)S(1)}, bf16[2,1152,128]{1,2,0:T(8,128)(2,1)}, u32[]{:S(2)}) copy-start(bf16[2,1152,128]{1,2,0:T(8,128)(2,1)} %get-tuple-element.304) | copy-start | bytes 1769476 | tf_op jit(solution)/shard_map/while
  180.0 2.8 %copy-start.6 = (f32[128,1]{0,1:T(1,128)S(1)}, f32[128,1]{0,1:T(1,128)}, u32[]{:S(2)}) copy-start(f32[128,1]{0,1:T(1,128)} %copy-done.5) | copy-start | bytes 1540 | tf_op jit(solution)/shard_map/while
  180.0 2.8 %copy-start.8 = (f32[8,64]{1,0:T(8,128)S(1)}, f32[8,64]{1,0:T(8,128)}, u32[]{:S(2)}) copy-start(f32[8,64]{1,0:T(8,128)} %copy-done.7) | copy-start | bytes 6148 | tf_op jit(solution)/shard_map/while
  (2 other events, 1.0 us)
